TPU v7x, 32 devices: a whole 2x2x4 slice. The times are simulated.
32 devices in a mesh: row: 4 (over y, x), col: 8 (over z, core).
Axes of the slice: x: 2, y: 2, z: 4, core: 2. Of those that a mesh axis runs over, the one named last changes fastest.
Arguments:
- tokens: bfloat16 [256, 12288], P('col', 'row'), may hold values from -6 to 6
- weight: bfloat16 [12288, 24576], P('row', 'col'), may hold values from -0.0546875 to 0.0546875
- bias: float32 [24576], P('col'), may hold values from -4 to 4
- cotangent: bfloat16 [256, 24576], P(None, 'col'), may hold values from -6 to 6
Outputs:
- hidden: bfloat16 [256, 24576], P('row', 'col')
- grad_tokens: bfloat16 [256, 12288], P('col', 'row')
- grad_weight: bfloat16 [12288, 24576], P('row', 'col')
- grad_bias: float32 [24576], P('col')
All inputs are finite; a program needn't handle non-finite values.
Results may differ from a plain program's by a relative error of at most 0.0055.
Values may be sent and summed in bfloat16 or wider, within the bound.
No kernel may reach another device: no remote copies, remote signals or barrier semaphores. Data moves between devices by JAX's collectives and lax.ppermute only.
A program may use at most 192 MiB of HBM per device.

v0:
```python
import math
import jax
import jax.numpy as jnp
from jax import lax
from jax.sharding import PartitionSpec as P


def activate(preact, cotangent):
    normal_cdf = 0.5 * (1.0 + jax.scipy.special.erf(preact / math.sqrt(2.0)))
    normal_pdf = jnp.exp(-0.5 * preact * preact) / math.sqrt(2.0 * math.pi)
    hidden = (preact * normal_cdf).astype(jnp.bfloat16)
    grad_pre = (cotangent.astype(jnp.float32) * (normal_cdf + preact * normal_pdf)).astype(
        jnp.bfloat16
    )
    return (hidden, grad_pre)


def body(tokens, weight, bias, cotangent):
    local_x = lax.all_gather(tokens, "col", axis=0, tiled=True)
    total_rows = local_x.shape[0]
    my_rows = total_rows // lax.axis_size("row")
    first_row = lax.axis_index("row") * my_rows
    partial_value = jnp.dot(local_x, weight, preferred_element_type=jnp.float32)
    preact = lax.psum(partial_value, "row") + bias
    all_hidden, full_grad = activate(preact, cotangent)
    hidden = lax.dynamic_slice_in_dim(all_hidden, first_row, my_rows, 0)
    grad_tokens = lax.psum_scatter(
        lax.dot_general(
            full_grad, weight, (((1,), (1,)), ((), ())), preferred_element_type=jnp.float32
        ),
        "col",
        scatter_dimension=0,
        tiled=True,
    ).astype(jnp.bfloat16)
    grad_weight = lax.dot_general(
        local_x, full_grad, (((0,), (0,)), ((), ())), preferred_element_type=jnp.float32
    ).astype(jnp.bfloat16)
    grad_bias = jnp.sum(full_grad.astype(jnp.float32), axis=0)
    return (hidden, grad_tokens, grad_weight, grad_bias)


def solution(mesh):
    placed = (P("col", "row"), P("row", "col"), P("col"), P(None, "col"))
    return jax.shard_map(
        body,
        mesh=mesh,
        in_specs=placed,
        out_specs=(P("row", "col"), P("col", "row"), P("row", "col"), P("col")),
        check_vma=False,
    )
```

profile of v0, /device:TPU:0, one launch (start us, length us, event | category | flops | bytes accessed | tf_op | source)
XLA Modules:
  0.0 199.8 jit_solution(12277951146830679832)
XLA Ops:
  7.2 0.0 all-gather.2.cloned.1.call-start
  7.2 0.7 all-gather.2.cloned.1.call-update
  7.9 0.0 all-reduce.2.cloned.1.call-start
  7.9 29.5 %all-gather.2.cloned.1.call-done = bf16[256,3072]{1,0:T(8,128)(2,1)} async-done(((bf16[32,3072]{1,0:T(8,128)(2,1)}), bf16[256,3072]{1,0:T(8,128)(2,1)}) %all-gather.2.cloned.1.call-update) | async-done | bytes 1572880 | tf_op jit(solution)/shard_map/all_gather | solution.py:19
  37.4 10.6 %fusion.8 = f32[256,3072]{1,0:T(8,128)} fusion(bf16[256,3072]{1,0:T(8,128)(2,1)} %all-gather.2.cloned.1.call-done, bf16[3072,3072]{1,0:T(8,128)(2,1)} %param.5), kind=kOutput, calls=%fused_computation.13 | convolution fusion | flops 4831838208 | bytes 23592960 | tf_op jit(solution)/shard_map/dot_general | solution.py:23
  48.0 0.0 copy-start.1
  48.0 0.0 copy-start.2
  48.0 0.0 all-reduce.2.cloned.1.call-update
  48.0 0.0 reduce-scatter.2.cloned.1.call-start
  48.1 86.8 %all-reduce.2.cloned.1.call-done = f32[256,3072]{1,0:T(8,128)} async-done(((f32[256,3072]{1,0:T(8,128)}), f32[256,3072]{1,0:T(8,128)}) %all-reduce.2.cloned.1.call-update) | async-done | bytes 3145744 | tf_op jit(solution)/shard_map/psum | solution.py:24
  134.9 0.0 copy-done.1
  134.9 0.0 copy-done.2
  134.9 5.4 %convert_reduce_fusion = (f32[3072]{0:T(1024)}, bf16[256,3072]{1,0:T(8,128)(2,1)S(1)}, f32[256,3072]{1,0:T(8,128)}, f32[256,3072]{1,0:T(8,128)}) fusion(bf16[256,3072]{1,0:T(8,128)(2,1)S(1)} %copy-done.1, f32[256,3072]{1,0:T(8,128)} %all-reduce.2.cloned.1.call-done, f32[3072]{0:T(1024)S(1)} %copy-done.2), kind=kLoop, calls=%fused_computation.8 | loop fusion | flops 11006976 | bytes 12607488 | tf_op jit(solution)/shard_map/reduce_sum | solution.py:38
  140.3 10.7 %fusion.9 = f32[256,3072]{1,0:T(8,128)} fusion(bf16[256,3072]{1,0:T(8,128)(2,1)S(1)} %get-tuple-element.9, bf16[3072,3072]{1,0:T(8,128)(2,1)} %param.5), kind=kOutput, calls=%fused_computation.14 | convolution fusion | flops 4831838208 | bytes 23592960 | tf_op jit(solution)/shard_map/dot_general | solution.py:28
  151.1 0.0 copy-start
  151.1 0.0 reduce-scatter.2.cloned.1.call-update
  151.1 1.4 copy-done
  152.5 9.2 %convert_bitcast_fusion = bf16[3072,3072]{0,1:T(8,128)(2,1)} fusion(bf16[256,3072]{1,0:T(8,128)(2,1)S(1)} %get-tuple-element.9, bf16[256,3072]{1,0:T(8,128)(2,1)S(1)} %copy-done), kind=kOutput, calls=%fused_computation | convolution fusion | flops 4841275392 | bytes 22020096 | tf_op jit(solution)/shard_map/dot_general | solution.py:35
  161.6 24.7 %copy.8 = bf16[3072,3072]{1,0:T(8,128)(2,1)} copy(bf16[3072,3072]{0,1:T(8,128)(2,1)} %convert_bitcast_fusion) | data formatting | bytes 37748736
  186.3 2.2 %fusion.6 = bf16[64,3072]{1,0:T(8,128)(2,1)} fusion(f32[256,3072]{1,0:T(8,128)} %get-tuple-element.10, s32[]{:T(128)S(6)} %select_n.3, f32[256,3072]{1,0:T(8,128)} %get-tuple-element.11), kind=kLoop, calls=%fused_computation.12 | loop fusion | flops 393216 | bytes 1966084 | tf_op jit(solution)/shard_map/convert_element_type | solution.py:11
  188.5 3.1 %reduce-scatter.2.cloned.1.call-done = f32[32,3072]{1,0:T(8,128)} async-done(((f32[256,3072]{1,0:T(8,128)}), f32[32,3072]{1,0:T(8,128)}) %reduce-scatter.2.cloned.1.call-update) | async-done | bytes 393232 | tf_op jit(solution)/shard_map/reduce_scatter | solution.py:27
  191.6 1.7 convert_element_type.24
Async XLA Ops:
  7.2 30.3 %all-gather.2.cloned.1.call-start = ((), (), s32[]{:S(2)}) async-start(), calls=%async_computation.1 | async-start | bytes 1769472 | tf_op jit(solution)/shard_map/all_gather | solution.py:19
  7.9 127.0 %all-reduce.2.cloned.1.call-start = ((), (), s32[]{:S(2)}) async-start(), calls=%async_computation.2 | async-start | bytes 6291456 | tf_op jit(solution)/shard_map/psum | solution.py:24
  48.0 86.9 %copy-start.1 = (bf16[256,3072]{1,0:T(8,128)(2,1)S(1)}, bf16[256,3072]{1,0:T(8,128)(2,1)}, u32[]{:S(2)}) copy-start(bf16[256,3072]{1,0:T(8,128)(2,1)} %param.7) | copy-start | bytes 4718596
  48.0 86.9 %copy-start.2 = (f32[3072]{0:T(1024)S(1)}, f32[3072]{0:T(1024)}, u32[]{:S(2)}) copy-start(f32[3072]{0:T(1024)} %param.6) | copy-start | bytes 36868
  48.0 143.6 %reduce-scatter.2.cloned.1.call-start = ((), (), s32[]{:S(2)}) async-start(), calls=%async_computation.3 | async-start | bytes 3538944 | tf_op jit(solution)/shard_map/reduce_scatter | solution.py:27
  151.1 1.4 copy-start
Sparse Core Ops, SparseCore 0:
  9.6 27.7 all-gather.1
  48.1 86.7 all-reduce.1
  151.2 40.3 reduce-scatter.1
where the time goes:
time: 201 us; the launch traced here: 200 us
  waiting for transfers between devices  120 us (60%)
  matrix products  30.4 us (15%)
  local copies, waits for them, and re-layouts  26 us (13%)
  between operations  13.8 us (7%)
  other arithmetic  9.32 us (5%)
    psum x1, waiting for transfers between devices, body(): preact = lax.psum(partial_value, 'row') + bias  86.8 us
    all_gather x1, waiting for transfers between devices, body(): local_x = lax.all_gather(tokens, 'col', axis=0, tiled=True)  29.5 us
    unnamed x7, local copies, waits for them, and re-layouts  26 us
    dot_general x1, matrix products, body(): lax.dot_general(full_grad, weight, (((1,), (1,)), ((), ())), preferred_el...  10.7 us
    dot_general x1, matrix products, body(): partial_value = jnp.dot(local_x, weight, preferred_element_type=jnp.float32)  10.6 us
    dot_general x1, matrix products, body(): lax.dot_general(local_x, full_grad, (((0,), (0,)), ((), ())), preferred_e...  9.17 us
    reduce_sum x1, other arithmetic, body(): grad_bias = jnp.sum(full_grad.astype(jnp.float32), axis=0)  5.43 us
  transfers between devices with their start and end apart: 3, of which 3 were waited for; matrix products, arithmetic and copies ran while one was open for 18% of the time, Pallas kernels for 0%

commit v1 on v0

--- a/solution.py
+++ b/solution.py
@@ -21,7 +21,7 @@
     my_rows = total_rows // lax.axis_size("row")
     first_row = lax.axis_index("row") * my_rows
     partial_value = jnp.dot(local_x, weight, preferred_element_type=jnp.float32)
-    preact = lax.psum(partial_value, "row") + bias
+    preact = jnp.sum(lax.all_gather(partial_value, "row"), axis=0) + bias
     all_hidden, full_grad = activate(preact, cotangent)
     hidden = lax.dynamic_slice_in_dim(all_hidden, first_row, my_rows, 0)
     grad_tokens = lax.psum_scatter(

time: 201 us -> 243 us (1.21)
  waiting for transfers between devices: 120 us -> 155 us
  other arithmetic: 9.32 us -> 15.2 us
    all_gather x0 -> x1, waiting for transfers between devices: none -> 122 us  [body(): preact = jnp.sum(lax.all_gather(partial_value, 'row'), axis=0) + bias]
    psum x1 -> x0, waiting for transfers between devices: 86.8 us -> none  [body(): preact = lax.psum(partial_value, 'row') + bias]
    reduce_sum x0 -> x1, other arithmetic: none -> 6.1 us  [body(): preact = jnp.sum(lax.all_gather(partial_value, 'row'), axis=0) + bias]
    unnamed x7 -> x9, local copies, waits for them, and re-layouts: 26 us -> 27.7 us
  transfers between devices with their start and end apart: 3 -> 3, of which waited for: 3 -> 3; matrix products, arithmetic and copies ran while one was open for 18% -> 15% of each run, Pallas kernels for 0% -> 0%
where the time goes in v1:
time: 243 us; the launch traced here: 242 us
  waiting for transfers between devices  155 us (64%)
  matrix products  30.6 us (13%)
  local copies, waits for them, and re-layouts  27.7 us (11%)
  other arithmetic  15.2 us (6%)
  between operations  13.8 us (6%)
    all_gather x1, waiting for transfers between devices, body(): preact = jnp.sum(lax.all_gather(partial_value, 'row'), axis=0) + bias  122 us
    all_gather x1, waiting for transfers between devices, body(): local_x = lax.all_gather(tokens, 'col', axis=0, tiled=True)  29.5 us
    unnamed x9, local copies, waits for them, and re-layouts  27.7 us
    dot_general x1, matrix products, body(): lax.dot_general(full_grad, weight, (((1,), (1,)), ((), ())), preferred_el...  10.7 us
    dot_general x1, matrix products, body(): partial_value = jnp.dot(local_x, weight, preferred_element_type=jnp.float32)  10.6 us
    dot_general x1, matrix products, body(): lax.dot_general(local_x, full_grad, (((0,), (0,)), ((), ())), preferred_e...  9.24 us
    reduce_sum x1, other arithmetic, body(): preact = jnp.sum(lax.all_gather(partial_value, 'row'), axis=0) + bias  6.1 us
    reduce_sum x1, other arithmetic, body(): grad_bias = jnp.sum(full_grad.astype(jnp.float32), axis=0)  5.2 us
  transfers between devices with their start and end apart: 3, of which 3 were waited for; matrix products, arithmetic and copies ran while one was open for 15% of the time, Pallas kernels for 0%

profile of v1, /device:TPU:0, one launch (start us, length us, event | category | flops | bytes accessed | tf_op | source)
XLA Modules:
  0.0 242.2 jit_solution(8334888431105292022)
XLA Ops:
  7.2 0.0 all-gather.4.cloned.1.call-start
  7.2 0.7 all-gather.4.cloned.1.call-update
  7.9 0.0 all-gather.6.cloned.1.call-start
  7.9 29.5 %all-gather.4.cloned.1.call-done = bf16[256,3072]{1,0:T(8,128)(2,1)} async-done(((bf16[32,3072]{1,0:T(8,128)(2,1)}), bf16[256,3072]{1,0:T(8,128)(2,1)}) %all-gather.4.cloned.1.call-update) | async-done | bytes 1572880 | tf_op jit(solution)/shard_map/all_gather | solution.py:19
  37.4 10.6 %fusion.8 = f32[256,3072]{1,0:T(8,128)} fusion(bf16[256,3072]{1,0:T(8,128)(2,1)} %all-gather.4.cloned.1.call-done, bf16[3072,3072]{1,0:T(8,128)(2,1)} %param.5), kind=kOutput, calls=%fused_computation.13 | convolution fusion | flops 4831838208 | bytes 23592960 | tf_op jit(solution)/shard_map/dot_general | solution.py:23
  48.0 0.0 all-gather.6.cloned.1.call-update
  48.1 0.0 reduce-scatter.2.cloned.1.call-start
  48.1 122.2 %all-gather.6.cloned.1.call-done = f32[1024,3072]{1,0:T(8,128)} async-done(((f32[256,3072]{1,0:T(8,128)}), f32[1024,3072]{1,0:T(8,128)}) %all-gather.6.cloned.1.call-update) | async-done | bytes 12582928 | tf_op jit(solution)/shard_map/all_gather | solution.py:24
  170.3 0.0 copy-start.3
  170.3 6.1 %reduce_sum.18 = f32[256,3072]{1,0:T(8,128)S(1)} reduce(f32[4,256,3072]{2,1,0:T(8,128)} %bitcast.9, f32[]{:T(128)} %constant.10.clone.1), dimensions={0}, to_apply=%region_0.0 | reduce | flops 2359296 | bytes 15728644 | tf_op jit(solution)/shard_map/reduce_sum | solution.py:24
  176.4 0.0 copy-done.3
  176.4 5.2 %convert_reduce_fusion = (f32[3072]{0:T(1024)}, bf16[256,3072]{1,0:T(8,128)(2,1)S(1)}, f32[256,3072]{1,0:T(8,128)}, f32[256,3072]{1,0:T(8,128)}) fusion(bf16[256,3072]{1,0:T(8,128)(2,1)} %param.7, f32[256,3072]{1,0:T(8,128)S(1)} %reduce_sum.18, f32[3072]{0:T(1024)S(1)} %copy-done.3), kind=kLoop, calls=%fused_computation.8 | loop fusion | flops 11006976 | bytes 12607488 | tf_op jit(solution)/shard_map/reduce_sum | solution.py:38
  181.6 0.0 copy-start
  181.6 1.1 copy-done
  182.7 10.7 %fusion.9 = f32[256,3072]{1,0:T(8,128)} fusion(bf16[256,3072]{1,0:T(8,128)(2,1)S(1)} %get-tuple-element.9, bf16[3072,3072]{1,0:T(8,128)(2,1)} %param.5), kind=kOutput, calls=%fused_computation.14 | convolution fusion | flops 4831838208 | bytes 23592960 | tf_op jit(solution)/shard_map/dot_general | solution.py:28
  193.4 0.0 copy-start.1
  193.5 0.0 reduce-scatter.2.cloned.1.call-update
  193.5 1.4 copy-done.1
  194.9 0.5 copy-done.2
  195.3 9.2 %convert_bitcast_fusion = bf16[3072,3072]{0,1:T(8,128)(2,1)} fusion(bf16[256,3072]{1,0:T(8,128)(2,1)S(1)} %copy-done.1, bf16[256,3072]{1,0:T(8,128)(2,1)S(1)} %copy-done.2), kind=kOutput, calls=%fused_computation | convolution fusion | flops 4841275392 | bytes 22020096 | tf_op jit(solution)/shard_map/dot_general | solution.py:35
  204.6 24.7 %copy.8 = bf16[3072,3072]{1,0:T(8,128)(2,1)} copy(bf16[3072,3072]{0,1:T(8,128)(2,1)} %convert_bitcast_fusion) | data formatting | bytes 37748736
  229.2 2.2 fusion.6
  231.4 2.5 %reduce-scatter.2.cloned.1.call-done = f32[32,3072]{1,0:T(8,128)} async-done(((f32[256,3072]{1,0:T(8,128)}), f32[32,3072]{1,0:T(8,128)}) %reduce-scatter.2.cloned.1.call-update) | async-done | bytes 393232 | tf_op jit(solution)/shard_map/reduce_scatter | solution.py:27
  234.0 1.7 convert_element_type.24
  (1 shorter events, 0.0 us)
Async XLA Ops:
  7.2 30.3 %all-gather.4.cloned.1.call-start = ((), (), s32[]{:S(2)}) async-start(), calls=%async_computation.1 | async-start | bytes 1769472 | tf_op jit(solution)/shard_map/all_gather | solution.py:19
  7.9 162.4 %all-gather.6.cloned.1.call-start = ((), (), s32[]{:S(2)}) async-start(), calls=%async_computation.3 | async-start | bytes 15728640 | tf_op jit(solution)/shard_map/all_gather | solution.py:24
  48.1 185.9 %reduce-scatter.2.cloned.1.call-start = ((), (), s32[]{:S(2)}) async-start(), calls=%async_computation.2 | async-start | bytes 3538944 | tf_op jit(solution)/shard_map/reduce_scatter | solution.py:27
  170.3 6.1 %copy-start.3 = (f32[3072]{0:T(1024)S(1)}, f32[3072]{0:T(1024)}, u32[]{:S(2)}) copy-start(f32[3072]{0:T(1024)} %param.6) | copy-start | bytes 36868
  181.6 1.1 copy-start
  193.4 1.4 copy-start.1
  193.5 1.9 copy-start.2
Sparse Core Ops, SparseCore 0:
  9.6 27.7 all-gather.3
  48.2 122.0 all-gather.5
  193.6 40.3 reduce-scatter.1
